TPU v7x, 512 devices: a whole 4x4x16 slice. The times are simulated.
512 devices in a mesh: dp: 4 (over y), seq: 16 (over z), section: 8 (over x, core).
Axes of the slice: x: 4, y: 4, z: 16, core: 2. Of those that a mesh axis runs over, the one named last changes fastest.
Arguments:
- signal: bfloat16 [4, 10240, 1280], P('dp', 'seq'), may hold values from -6 to 6
- kernel: bfloat16 [1536, 5, 1280], P('section'), may hold values from -0.078125 to 0.078125
- trunk_grad: bfloat16 [4, 5120, 1536], P('dp', ('seq', 'section')), may hold values from -24 to 24
Outputs:
- weight_grad: float32 [1536, 5, 1280], P(('section', 'seq'))
- input_grad: bfloat16 [4, 1280, 10240], P('dp', 'section', 'seq')
All inputs are finite; a program needn't handle non-finite values.
Results may differ from a plain program's by a relative error of at most 0.019.
Values may be sent and summed in bfloat16 or wider, within the bound.
No kernel may reach another device: no remote copies, remote signals or barrier semaphores. Data moves between devices by JAX's collectives and lax.ppermute only.
A program may use at most 64 MiB of HBM per device.

v0:
```python
import jax
import jax.numpy as jnp
from jax import lax
from jax.sharding import PartitionSpec as P


def extended(block, sides, width):
    for axis, dim in sides:
        count = lax.axis_size(axis)
        forward = [(i, i + 1) for i in range(count - 1)]
        backward = [(target, source) for source, target in forward]
        low = lax.ppermute(
            lax.slice_in_dim(block, block.shape[dim] - width, None, axis=dim), axis, forward
        )
        high = lax.ppermute(lax.slice_in_dim(block, 0, width, axis=dim), axis, backward)
        block = jnp.concatenate([low, block, high], axis=dim)
    return block


def gelu_slope(values):
    normal_cdf = 0.5 * (1.0 + jax.scipy.special.erf(values * 0.7071067811865476))
    density = jnp.exp(-0.5 * values * values) * 0.3989422804014327
    return normal_cdf + values * density


def convolve(padded, kernel, out_rows):
    linear = jnp.einsum(
        "lc,oc->lo", padded[0:out_rows], kernel[:, 0, :], preferred_element_type=jnp.float32
    )
    for offset in range(1, kernel.shape[1]):
        linear = linear + jnp.einsum(
            "lc,oc->lo",
            padded[offset : offset + out_rows],
            kernel[:, offset, :],
            preferred_element_type=jnp.float32,
        )
    return linear


def shards(signal, kernel, trunk_grad):
    local_signal = signal[0]
    length = local_signal.shape[0]
    taps_count = kernel.shape[1]
    pooled = lax.all_to_all(trunk_grad, "section", split_axis=2, concat_axis=1, tiled=True)[0]
    padded = extended(local_signal, (("seq", 0),), 2)
    linear = convolve(padded, kernel, length)
    grad_hidden = 0.5 * jnp.repeat(pooled.astype(jnp.float32), 2, axis=0)
    grad_pre = (grad_hidden * gelu_slope(linear)).astype(jnp.bfloat16)
    grad_ext = extended(grad_pre, (("seq", 0),), 2)
    grad_middle = grad_ext[2 : 2 + length]
    taps = []
    for offset in range(taps_count):
        taps.append(
            jnp.einsum(
                "lo,lc->oc",
                grad_middle,
                padded[offset : offset + length],
                preferred_element_type=jnp.float32,
            )
        )
    weight_rows = lax.psum_scatter(
        jnp.stack(taps, axis=1).astype(jnp.bfloat16), "seq", scatter_dimension=0, tiled=True
    )
    weight_grad = lax.psum(weight_rows, "dp").astype(jnp.float32)
    summed = jnp.einsum(
        "lo,oc->cl", grad_ext[4 : 4 + length], kernel[:, 0, :], preferred_element_type=jnp.float32
    )
    for offset in range(1, taps_count):
        summed = summed + jnp.einsum(
            "lo,oc->cl",
            grad_ext[4 - offset : 4 - offset + length],
            kernel[:, offset, :],
            preferred_element_type=jnp.float32,
        )
    input_rows = lax.psum_scatter(
        summed.astype(jnp.bfloat16), "section", scatter_dimension=0, tiled=True
    )
    return (weight_grad, input_rows[None])


def solution(mesh):
    return jax.shard_map(
        shards,
        mesh=mesh,
        in_specs=(
            P("dp", "seq", None),
            P("section", None, None),
            P("dp", ("seq", "section"), None),
        ),
        out_specs=(P(("section", "seq"), None, None), P("dp", "section", "seq")),
        check_vma=False,
    )
```

profile of v0, /device:TPU:2, one launch (start us, length us, event | category | flops | bytes accessed | tf_op | source)
XLA Modules:
  0.0 269.3 jit_solution(15086313837585822264)
XLA Ops:
  8.0 0.9 slice_bitcast_fusion.1
  8.9 3.8 %collective-permute-start = (bf16[2,1280]{1,0:T(2,128)(2,1)S(1)}, bf16[2,1280]{1,0:T(2,128)(2,1)S(1)}, u32[]{:S(2)}, u32[]{:S(2)}) collective-permute-start(bf16[2,1280]{1,0:T(2,128)(2,1)S(1)} %get-tuple-element.8), channel_id=1, source_target_pairs={{0,8},{8,16},{16,24},{24,32},{32,40},{40,48},{48,56},{56,64},{64,7... | collective-permute-start | bytes 15368 | tf_op jit(solution)/shard_map/ppermute | solution.py:12
  12.7 1.3 collective-permute-start.1
  14.0 1.9 copy.9
  16.0 0.5 broadcast.19
  16.5 9.6 %reduce = bf16[1536,40]{1,0:T(8,128)(2,1)} reduce(bf16[1536,1,40]{2,1,0:T(2,128)(2,1)S(1)} %bitcast.76, bf16[]{:T(256)} %broadcast.19), dimensions={1}, to_apply=%bitcast.67.reduce_sub_computation | reduce | bytes 245762
  26.0 2.2 reshape.21
  28.3 6.7 %all-to-all-start = ((bf16[8,2,3840]{2,1,0:T(2,128)(2,1)}), bf16[8,2,3840]{2,1,0:T(2,128)(2,1)S(1)}, u32[]{:S(2)}, u32[]{:S(2)}) async-start(bf16[8,2,3840]{2,1,0:T(2,128)(2,1)} %reshape.21), calls=%async_computation | async-start | bytes 245760 | tf_op jit(solution)/shard_map/all_to_all | solution.py:44
  34.9 2.2 fusion.33
  37.2 0.7 fusion.18
  37.9 1.5 fusion.16
  39.4 1.5 fusion.19
  40.9 1.2 reshape.22
  42.1 0.9 convert_multiply_fusion
  43.0 0.3 copy.10
  43.3 0.2 broadcast_in_dim.6
  43.5 0.5 mul.50
  44.0 0.2 copy.11
  44.2 0.2 copy-done.3
  44.4 2.3 fusion.25
  46.8 0.6 fusion.5
  47.4 0.6 fusion.7
  48.0 0.6 fusion.9
  48.6 0.6 fusion.11
  49.2 0.6 fusion.13
  49.9 1.4 copy-done
  51.3 0.0 all-reduce.6.cloned.1.call-update
  51.3 0.0 all-reduce.4.cloned.1.call-start
  51.4 1.3 dynamic-slice
  53.3 0.1 fusion.72
  53.4 1.3 collective-permute-start.2
  54.7 1.7 fusion.31
  56.4 5.2 %collective-permute-start.3 = (bf16[2,192]{0,1:T(8,128)(2,1)S(1)}, bf16[2,192]{0,1:T(8,128)(2,1)S(1)}, u32[]{:S(2)}, u32[]{:S(2)}) collective-permute-start(bf16[2,192]{0,1:T(8,128)(2,1)S(1)} %get-tuple-element.11), channel_id=1, source_target_pairs={{0,8},{8,16},{16,24},{24,32},{32,40},{40,48},{48,56},{56,64},{64,7... | collective-permute-start | bytes 2312 | tf_op jit(solution)/shard_map/ppermute | solution.py:12
  61.6 1.8 fusion.35
  63.4 0.6 copy-done.5
  64.0 1.8 fusion.26
  65.8 3.5 %fusion.1 = f32[640,1280]{1,0:T(8,128)} fusion(f32[640,1280]{1,0:T(8,128)S(1)} %fusion.31, f32[640,1280]{1,0:T(8,128)S(1)} %fusion.35, bf16[192,5,1280]{2,0,1:T(8,128)(2,1)} %param.4, bf16[640,192]{0,1:T(8,128)(2,1)S(1)} %fusion.25, bf16[2,192]{0,1:T(8,128)(2,1)S(1)} %collective-permute-done.2), kind=kOutput, calls=%fused_computation.3 | convolution fusion | flops 316702720 | bytes 10568448 | tf_op jit(solution)/shard_map/lo,oc->cl/dot_general | solution.py:65
  69.3 133.3 %all-reduce.6.cloned.1.call-done = bf16[192,5,1280]{2,0,1:T(8,128)(2,1)} async-done(((bf16[192,5,1280]{2,0,1:T(8,128)(2,1)}), bf16[192,5,1280]{2,0,1:T(8,128)(2,1)}) %all-reduce.6.cloned.1.call-update) | async-done | bytes 2457616
  202.6 1.7 constant_dynamic-slice_fusion
  204.3 0.0 all-reduce.4.cloned.1.call-update
  204.3 0.0 reduce-scatter.5.cloned.1.call-start
  204.4 4.1 %fusion.3 = bf16[1280,640]{0,1:T(8,128)(2,1)} fusion(f32[640,1280]{1,0:T(8,128)S(1)} %fusion.26, f32[640,1280]{1,0:T(8,128)} %fusion.1, bf16[192,5,1280]{2,0,1:T(8,128)(2,1)} %param.4, bf16[2,192]{0,1:T(8,128)(2,1)} %copy-done.5, bf16[640,192]{0,1:T(8,128)(2,1)S(1)} %fusion.25), kind=kOutput, calls=%fused_computation.5 | convolution fusion | flops 317521920 | bytes 8978432 | tf_op jit(solution)/shard_map/lo,oc->cl/dot_general | solution.py:69
  208.4 3.5 %copy.15 = bf16[1280,640]{1,0:T(8,128)(2,1)} copy(bf16[1280,640]{0,1:T(8,128)(2,1)} %fusion.3) | data formatting | bytes 3276800
  212.0 0.0 reduce-scatter.5.cloned.1.call-update
  212.0 46.3 %all-reduce.4.cloned.1.call-done = bf16[12,5,1280]{2,0,1:T(8,128)(2,1)} async-done(((bf16[12,5,1280]{2,0,1:T(8,128)(2,1)}), bf16[12,5,1280]{2,0,1:T(8,128)(2,1)}) %all-reduce.4.cloned.1.call-update) | async-done | bytes 153616 | tf_op jit(solution)/shard_map/psum | solution.py:64
  258.3 1.7 convert_element_type.16
  260.0 1.1 copy.16
  261.1 0.8 copy.12
  (16 shorter events, 0.0 us)
Async XLA Ops:
  8.0 26.9 %copy-start.1 = (bf16[192,5,1280]{2,0,1:T(8,128)(2,1)S(1)}, bf16[192,5,1280]{2,0,1:T(8,128)(2,1)}, u32[]{:S(2)}) copy-start(bf16[192,5,1280]{2,0,1:T(8,128)(2,1)} %param.4) | copy-start | bytes 7372804
  8.9 28.3 %collective-permute-start = (bf16[2,1280]{1,0:T(2,128)(2,1)S(1)}, bf16[2,1280]{1,0:T(2,128)(2,1)S(1)}, u32[]{:S(2)}, u32[]{:S(2)}) collective-permute-start(bf16[2,1280]{1,0:T(2,128)(2,1)S(1)} %get-tuple-element.8), channel_id=1, source_target_pairs={{0,8},{8,16},{16,24},{24,32},{32,40},{40,48},{48,56},{56,64},{64,7... | collective-permute-start | bytes 15368 | tf_op jit(solution)/shard_map/ppermute | solution.py:12
  12.7 26.7 %collective-permute-start.1 = (bf16[2,1280]{1,0:T(2,128)(2,1)S(1)}, bf16[2,1280]{1,0:T(2,128)(2,1)S(1)}, u32[]{:S(2)}, u32[]{:S(2)}) collective-permute-start(bf16[2,1280]{1,0:T(2,128)(2,1)S(1)} %get-tuple-element.9), channel_id=1, source_target_pairs={{8,0},{16,8},{24,16},{32,24},{40,32},{48,40},{56,48},{64,56},{72,6... | collective-permute-start | bytes 15368 | tf_op jit(solution)/shard_map/ppermute | solution.py:15
  28.3 12.7 %all-to-all-start = ((bf16[8,2,3840]{2,1,0:T(2,128)(2,1)}), bf16[8,2,3840]{2,1,0:T(2,128)(2,1)S(1)}, u32[]{:S(2)}, u32[]{:S(2)}) async-start(bf16[8,2,3840]{2,1,0:T(2,128)(2,1)} %reshape.21), calls=%async_computation | async-start | bytes 245760 | tf_op jit(solution)/shard_map/all_to_all | solution.py:44
  34.9 167.7 %all-reduce.6.cloned.1.call-start = ((), (), s32[]{:S(2)}) async-start(), calls=%async_computation.4 | async-start | bytes 4915200
  34.9 2.3 copy-start.2
  43.0 1.4 copy-start.3
  44.4 2.3 copy-start.4
  49.9 1.5 copy-start
  51.3 206.9 %all-reduce.4.cloned.1.call-start = ((), (), s32[]{:S(2)}) async-start(), calls=%async_computation.2 | async-start | bytes 409600 | tf_op jit(solution)/shard_map/psum | solution.py:64
  53.4 8.2 %collective-permute-start.2 = (bf16[2,192]{0,1:T(8,128)(2,1)S(1)}, bf16[2,192]{0,1:T(8,128)(2,1)S(1)}, u32[]{:S(2)}, u32[]{:S(2)}) collective-permute-start(bf16[2,192]{0,1:T(8,128)(2,1)S(1)} %get-tuple-element.10), channel_id=1, source_target_pairs={{8,0},{16,8},{24,16},{32,24},{40,32},{48,40},{56,48},{64,56},{72,6... | collective-permute-start | bytes 2312 | tf_op jit(solution)/shard_map/ppermute | solution.py:15
  56.4 7.0 %collective-permute-start.3 = (bf16[2,192]{0,1:T(8,128)(2,1)S(1)}, bf16[2,192]{0,1:T(8,128)(2,1)S(1)}, u32[]{:S(2)}, u32[]{:S(2)}) collective-permute-start(bf16[2,192]{0,1:T(8,128)(2,1)S(1)} %get-tuple-element.11), channel_id=1, source_target_pairs={{0,8},{8,16},{16,24},{24,32},{32,40},{40,48},{48,56},{56,64},{64,7... | collective-permute-start | bytes 2312 | tf_op jit(solution)/shard_map/ppermute | solution.py:12
  63.4 0.6 copy-start.5
  204.3 55.7 %reduce-scatter.5.cloned.1.call-start = ((), (), s32[]{:S(2)}) async-start(), calls=%async_computation.3 | async-start | bytes 1843200
Sparse Core Ops, SparseCore 0:
  51.5 151.0 all-reduce.5
  205.5 52.7 all-reduce.3
Sparse Core Ops, SparseCore 1:
  212.1 33.1 reduce-scatter.4
where the time goes:
time: 270 us; the launch traced here: 269 us
  waiting for transfers between devices  180 us (67%)
  matrix products  24.2 us (9%)
  local copies, waits for them, and re-layouts  18.7 us (7%)
  starting transfers between devices  18.3 us (7%)
  between operations  16.4 us (6%)
  other arithmetic  12.1 us (4%)
    unnamed x5, waiting for transfers between devices  133 us
    psum x1, waiting for transfers between devices, shards(): weight_grad = lax.psum(weight_rows, 'dp').astype(jnp.float32)  46.3 us
    unnamed x21, local copies, waits for them, and re-layouts  16.5 us
    unnamed x1, other arithmetic  9.56 us
    dot_general x4, matrix products, shards(): jnp.einsum('lo,oc->cl', grad_ext[4 - offset:4 - offset + length], kernel[...  9.31 us
    ppermute x2, starting transfers between devices, extended(): lax.ppermute(lax.slice_in_dim(block, block.shape[dim] - width, None, axis...  9 us
    dot_general x4, matrix products, convolve(): jnp.einsum('lc,oc->lo', padded[offset:offset + out_rows], kernel[:, offse...  6.78 us
    all_to_all x1, starting transfers between devices, shards(): lax.all_to_all(trunk_grad, 'section', split_axis=2, concat_axis=1, tiled=...  6.65 us
  transfers between devices with their start and end apart: 8, of which 2 were waited for; matrix products, arithmetic and copies ran while one was open for 15% of the time, Pallas kernels for 0%

commit v1 on v0

--- a/solution.py
+++ b/solution.py
@@ -61,7 +61,7 @@
     weight_rows = lax.psum_scatter(
         jnp.stack(taps, axis=1).astype(jnp.bfloat16), "seq", scatter_dimension=0, tiled=True
     )
-    weight_grad = lax.psum(weight_rows, "dp").astype(jnp.float32)
+    weight_grad = jnp.sum(lax.all_gather(weight_rows, "dp"), axis=0).astype(jnp.float32)
     summed = jnp.einsum(
         "lo,oc->cl", grad_ext[4 : 4 + length], kernel[:, 0, :], preferred_element_type=jnp.float32
     )

time: 270 us -> 229 us (0.85)
  waiting for transfers between devices: 180 us -> 134 us
  blocking collectives: 0 us -> 14 us
  matrix products: 24.2 us -> 17.1 us
    psum x1 -> x0, waiting for transfers between devices: 46.3 us -> none  [shards(): weight_grad = lax.psum(weight_rows, 'dp').astype(jnp.float32)]
    all_gather x0 -> x1, blocking collectives: none -> 14 us  [shards(): lax.all_gather(weight_rows, 'dp')]
    dot_general x4, matrix products: 9.31 us -> 4.98 us  [shards(): jnp.einsum('lo,oc->cl', grad_ext[4 - offset:4 - offset + length], kernel[...]
    dot_general x1, matrix products: 3.49 us -> 0.78 us  [shards(): jnp.einsum('lo,oc->cl', grad_ext[4:4 + length], kernel[:, 0, :], preferre...]
    unnamed x5 -> x4, waiting for transfers between devices: 133 us -> 134 us
  transfers between devices with their start and end apart: 8 -> 7, of which waited for: 2 -> 2; matrix products, arithmetic and copies ran while one was open for 15% -> 14% of each run, Pallas kernels for 0% -> 0%
where the time goes in v1:
time: 229 us; the launch traced here: 228 us
  waiting for transfers between devices  134 us (59%)
  starting transfers between devices  18.4 us (8%)
  matrix products  17.1 us (7%)
  between operations  16.4 us (7%)
  local copies, waits for them, and re-layouts  16.2 us (7%)
  blocking collectives  14 us (6%)
  other arithmetic  11.5 us (5%)
    unnamed x4, waiting for transfers between devices  134 us
    all_gather x1, blocking collectives, shards(): lax.all_gather(weight_rows, 'dp')  14 us
    unnamed x21, local copies, waits for them, and re-layouts  13.9 us
    unnamed x1, other arithmetic  9.56 us
    ppermute x2, starting transfers between devices, extended(): lax.ppermute(lax.slice_in_dim(block, block.shape[dim] - width, None, axis...  8.99 us
    dot_general x4, matrix products, convolve(): jnp.einsum('lc,oc->lo', padded[offset:offset + out_rows], kernel[:, offse...  6.76 us
    all_to_all x1, starting transfers between devices, shards(): lax.all_to_all(trunk_grad, 'section', split_axis=2, concat_axis=1, tiled=...  6.65 us
    dot_general x4, matrix products, shards(): jnp.einsum('lo,oc->cl', grad_ext[4 - offset:4 - offset + length], kernel[...  4.98 us
  transfers between devices with their start and end apart: 7, of which 2 were waited for; matrix products, arithmetic and copies ran while one was open for 14% of the time, Pallas kernels for 0%

profile of v1, /device:TPU:2, one launch (start us, length us, event | category | flops | bytes accessed | tf_op | source)
XLA Modules:
  0.0 228.1 jit_solution(15505607316703813991)
XLA Ops:
  8.0 0.9 slice_bitcast_fusion.1
  8.9 3.8 %collective-permute-start = (bf16[2,1280]{1,0:T(2,128)(2,1)S(1)}, bf16[2,1280]{1,0:T(2,128)(2,1)S(1)}, u32[]{:S(2)}, u32[]{:S(2)}) collective-permute-start(bf16[2,1280]{1,0:T(2,128)(2,1)S(1)} %get-tuple-element.8), channel_id=1, source_target_pairs={{0,8},{8,16},{16,24},{24,32},{32,40},{40,48},{48,56},{56,64},{64,7... | collective-permute-start | bytes 15368 | tf_op jit(solution)/shard_map/ppermute | solution.py:12
  12.7 1.3 collective-permute-start.1
  14.0 1.9 copy.9
  16.0 0.5 broadcast.19
  16.5 9.6 %reduce.1 = bf16[1536,40]{1,0:T(8,128)(2,1)} reduce(bf16[1536,1,40]{2,1,0:T(2,128)(2,1)S(1)} %bitcast.78, bf16[]{:T(256)} %broadcast.19), dimensions={1}, to_apply=%bitcast.68.reduce_sub_computation | reduce | bytes 245762
  26.0 2.2 reshape.22
  28.3 6.7 %all-to-all-start = ((bf16[8,2,3840]{2,1,0:T(2,128)(2,1)}), bf16[8,2,3840]{2,1,0:T(2,128)(2,1)S(1)}, u32[]{:S(2)}, u32[]{:S(2)}) async-start(bf16[8,2,3840]{2,1,0:T(2,128)(2,1)} %reshape.22), calls=%async_computation | async-start | bytes 245760 | tf_op jit(solution)/shard_map/all_to_all | solution.py:44
  34.9 2.2 fusion.33
  37.2 0.7 fusion.18
  37.9 1.5 fusion.16
  39.4 1.5 fusion.19
  40.9 1.2 reshape.23
  42.1 0.9 convert_multiply_fusion
  43.0 0.3 copy.10
  43.3 0.2 broadcast_in_dim.6
  43.5 0.5 mul.50
  44.0 0.2 copy.11
  44.2 0.2 copy-done.4
  44.4 2.3 %fusion.25 = bf16[640,192]{0,1:T(8,128)(2,1)S(1)} fusion(f32[640,192]{0,1:T(8,128)S(1)} %copy.11, f32[640,192]{0,1:T(8,128)} %fusion.19, f32[640,192]{0,1:T(8,128)} %fusion.16, bf16[192,5,1280]{2,0,1:T(8,128)(2,1)} %param.4, bf16[640,1280]{1,0:T(8,128)(2,1)S(1)} %bitcast.83, bf16[2,1280]{1,0:T(2,128)(2,1)S(1)} %collective-permute-done.1), kind=kOutput, calls=%fused_computation.42 | convolution fusion | flops 319324160 | bytes 3855360 | tf_op jit(solution)/shard_map/lc,oc->lo/dot_general | solution.py:31
  46.8 0.6 fusion.5
  47.4 0.6 fusion.7
  48.0 0.6 fusion.9
  48.6 0.6 fusion.11
  49.2 0.6 fusion.13
  49.9 1.4 copy-done
  51.3 0.0 all-reduce.3.cloned.1.call-update
  51.4 0.0 reduce-scatter.5.cloned.1.call-start
  51.4 0.1 fusion.72
  51.5 1.4 collective-permute-start.2
  52.9 1.7 fusion.31
  54.6 5.2 %collective-permute-start.3 = (bf16[2,192]{0,1:T(8,128)(2,1)S(1)}, bf16[2,192]{0,1:T(8,128)(2,1)S(1)}, u32[]{:S(2)}, u32[]{:S(2)}) collective-permute-start(bf16[2,192]{0,1:T(8,128)(2,1)S(1)} %get-tuple-element.11), channel_id=1, source_target_pairs={{0,8},{8,16},{16,24},{24,32},{32,40},{40,48},{48,56},{56,64},{64,7... | collective-permute-start | bytes 2312 | tf_op jit(solution)/shard_map/ppermute | solution.py:12
  59.8 0.8 fusion.35
  60.5 1.0 collective-permute-done.3
  61.5 0.7 fusion.26
  62.3 0.8 fusion.1
  63.0 1.8 fusion.3
  64.9 2.2 copy.18
  67.1 0.0 reduce-scatter.5.cloned.1.call-update
  67.1 1.3 dynamic-slice
  69.0 133.5 %all-reduce.3.cloned.1.call-done = bf16[192,5,1280]{2,0,1:T(8,128)(2,1)} async-done(((bf16[192,5,1280]{2,0,1:T(8,128)(2,1)}), bf16[192,5,1280]{2,0,1:T(8,128)(2,1)}) %all-reduce.3.cloned.1.call-update) | async-done | bytes 2457616
  202.5 1.0 constant_dynamic-slice_fusion
  203.5 0.1 copy.12
  203.6 14.0 %all-gather = bf16[48,5,1280]{2,1,0:T(8,128)(2,1)S(1)} all-gather(bf16[12,5,1280]{2,1,0:T(8,128)(2,1)S(1)} %copy.12), channel_id=2, replica_groups=mesh['dp'=4,'seq'=16,'section'=8] {'dp'}, dimensions={0}, use_global_device_ids=true | all-gather | bytes 768000 | tf_op jit(solution)/shard_map/all_gather | solution.py:64
  217.6 0.3 reduce_sum.12
  217.9 0.8 copy_convert_fusion
  218.7 1.1 copy.19
  219.8 0.8 copy.14
  (16 shorter events, 0.0 us)
Async XLA Ops:
  8.0 26.9 %copy-start.1 = (bf16[192,5,1280]{2,0,1:T(8,128)(2,1)S(1)}, bf16[192,5,1280]{2,0,1:T(8,128)(2,1)}, u32[]{:S(2)}) copy-start(bf16[192,5,1280]{2,0,1:T(8,128)(2,1)} %param.4) | copy-start | bytes 7372804
  8.9 28.3 %collective-permute-start = (bf16[2,1280]{1,0:T(2,128)(2,1)S(1)}, bf16[2,1280]{1,0:T(2,128)(2,1)S(1)}, u32[]{:S(2)}, u32[]{:S(2)}) collective-permute-start(bf16[2,1280]{1,0:T(2,128)(2,1)S(1)} %get-tuple-element.8), channel_id=1, source_target_pairs={{0,8},{8,16},{16,24},{24,32},{32,40},{40,48},{48,56},{56,64},{64,7... | collective-permute-start | bytes 15368 | tf_op jit(solution)/shard_map/ppermute | solution.py:12
  12.7 26.7 %collective-permute-start.1 = (bf16[2,1280]{1,0:T(2,128)(2,1)S(1)}, bf16[2,1280]{1,0:T(2,128)(2,1)S(1)}, u32[]{:S(2)}, u32[]{:S(2)}) collective-permute-start(bf16[2,1280]{1,0:T(2,128)(2,1)S(1)} %get-tuple-element.9), channel_id=1, source_target_pairs={{8,0},{16,8},{24,16},{32,24},{40,32},{48,40},{56,48},{64,56},{72,6... | collective-permute-start | bytes 15368 | tf_op jit(solution)/shard_map/ppermute | solution.py:15
  28.3 12.7 %all-to-all-start = ((bf16[8,2,3840]{2,1,0:T(2,128)(2,1)}), bf16[8,2,3840]{2,1,0:T(2,128)(2,1)S(1)}, u32[]{:S(2)}, u32[]{:S(2)}) async-start(bf16[8,2,3840]{2,1,0:T(2,128)(2,1)} %reshape.22), calls=%async_computation | async-start | bytes 245760 | tf_op jit(solution)/shard_map/all_to_all | solution.py:44
  34.9 167.6 %all-reduce.3.cloned.1.call-start = ((), (), s32[]{:S(2)}) async-start(), calls=%async_computation.3 | async-start | bytes 4915200
  34.9 2.3 copy-start.3
  43.0 1.4 copy-start.4
  44.4 2.3 %copy-start.5 = (bf16[1,640,1280]{2,1,0:T(8,128)(2,1)S(1)}, bf16[1,640,1280]{2,1,0:T(8,128)(2,1)}, u32[]{:S(2)}) copy-start(bf16[1,640,1280]{2,1,0:T(8,128)(2,1)} %param.3) | copy-start | bytes 4915204
  49.9 1.4 copy-start
  51.3 8.4 %copy-start.2 = (bf16[192,5,1280]{2,0,1:T(8,128)(2,1)S(1)}, bf16[192,5,1280]{2,0,1:T(8,128)(2,1)}, u32[]{:S(2)}) copy-start(bf16[192,5,1280]{2,0,1:T(8,128)(2,1)} %param.4) | copy-start | bytes 7372804
  51.4 167.4 %reduce-scatter.5.cloned.1.call-start = ((), (), s32[]{:S(2)}) async-start(), calls=%async_computation.2 | async-start | bytes 1843200
  51.5 8.3 %collective-permute-start.2 = (bf16[2,192]{0,1:T(8,128)(2,1)S(1)}, bf16[2,192]{0,1:T(8,128)(2,1)S(1)}, u32[]{:S(2)}, u32[]{:S(2)}) collective-permute-start(bf16[2,192]{0,1:T(8,128)(2,1)S(1)} %get-tuple-element.10), channel_id=1, source_target_pairs={{8,0},{16,8},{24,16},{32,24},{40,32},{48,40},{56,48},{64,56},{72,6... | collective-permute-start | bytes 2312 | tf_op jit(solution)/shard_map/ppermute | solution.py:15
  54.6 6.9 %collective-permute-start.3 = (bf16[2,192]{0,1:T(8,128)(2,1)S(1)}, bf16[2,192]{0,1:T(8,128)(2,1)S(1)}, u32[]{:S(2)}, u32[]{:S(2)}) collective-permute-start(bf16[2,192]{0,1:T(8,128)(2,1)S(1)} %get-tuple-element.11), channel_id=1, source_target_pairs={{0,8},{8,16},{16,24},{24,32},{32,40},{40,48},{48,56},{56,64},{64,7... | collective-permute-start | bytes 2312 | tf_op jit(solution)/shard_map/ppermute | solution.py:12
Sparse Core Ops, SparseCore 0:
  51.5 151.0 all-reduce.2
Sparse Core Ops, SparseCore 1:
  67.2 43.2 reduce-scatter.4
